TPU v7x, 128 devices: a whole 4x4x4 slice. The times are simulated.
128 devices in a mesh: seq: 32 (over x, y, core), fsdp: 4 (over z).
Axes of the slice: x: 4, y: 4, z: 4, core: 2. Of those that a mesh axis runs over, the one named last changes fastest.
Arguments:
- patches: bfloat16 [32768, 1280], P(('seq', 'fsdp')), may hold values from -6 to 6
- vis_index: int32 [32768], P(('seq', 'fsdp')), may hold values from 0 to 131071, as said below
- kv_list: int32 [256, 16], P(('seq', 'fsdp')), may hold values from 0 to 255, as said below
- kv_count: int32 [256], P(('seq', 'fsdp')), may hold values from 1 to 16, as said below
- global_tiles: int32 [2], replicated, may hold values from 0 to 255
- frame_table: bfloat16 [256, 1280], replicated, may hold values from -3 to 3
- space_table: bfloat16 [512, 1280], replicated, may hold values from -3 to 3
- ln_gain: bfloat16 [1280], replicated, may hold values from 0.25 to 1.75
- ln_bias: bfloat16 [1280], replicated, may hold values from -3 to 3
- w_qkv: bfloat16 [1280, 3840], P('fsdp')
- w_out: bfloat16 [1280, 1280], P('fsdp'), may hold values from -1.25 to 1.25
Outputs:
- attended: bfloat16 [32768, 1280], P(('seq', 'fsdp'))
Inputs may be any that keep to these rules, and one draw needn't show every extreme that they name: `vis_index`: exactly one visible position in each aligned group of four; strictly increasing. `kv_list`: the first entry of query tile i is i itself; entries may repeat; every entry t satisfies |t // 8 - i // 8| <= 2. Over all entries of an aligned run of 2 query tiles, the tiles that lie in any one group other than the run's own group (group = tile // 8) number at most 3 distinct ones, and exactly 3 for every such group within two of the run's own. On every device at least one query tile has kv_count = 16.
All inputs are finite; a program needn't handle non-finite values.
Results may differ from a plain program's by a relative error of at most 0.0065.
Values may be sent and summed in bfloat16 or wider, within the bound.
No kernel may reach another device: no remote copies, remote signals or barrier semaphores. Data moves between devices by JAX's collectives and lax.ppermute only.
A program may use at most 192 MiB of HBM per device.

v0:
```python
import jax
import jax.numpy as jnp
from jax import lax
from jax.sharding import PartitionSpec as P

HEADS = 16
TILE = 128
KT = 16
GLOBAL = 2
PATCHES = 512
NEAR = 3
REACH = (-2, -1, 1, 2)


def passed_along(block, axis, distance):
    devices = range(lax.axis_size(axis))
    route = [(i - distance, i) for i in devices if i - distance in devices]
    return lax.ppermute(block, axis, route)


def layer_norm(stream, ln_gain, ln_bias):
    stream32 = stream.astype(jnp.float32)
    mean_val = jnp.mean(stream32, axis=-1, keepdims=True)
    centred = stream32 - mean_val
    variance = jnp.mean(centred * centred, axis=-1, keepdims=True)
    scaled = centred * lax.rsqrt(variance + 1e-06)
    return (scaled * ln_gain.astype(jnp.float32) + ln_bias.astype(jnp.float32)).astype(jnp.bfloat16)


def embed(patches, vis_index, frame_table, space_table):
    frame_ids = vis_index // PATCHES
    patch_ids = vis_index % PATCHES
    return (
        patches.astype(jnp.float32)
        + frame_table[frame_ids].astype(jnp.float32)
        + space_table[patch_ids].astype(jnp.float32)
    ).astype(jnp.bfloat16)


def near_tiles(entries, group, group_tiles):
    cand = group * group_tiles + jnp.arange(group_tiles, dtype=jnp.int32)
    named = jnp.any(entries.reshape(-1, 1) == cand[None, :], axis=0)
    rank = jnp.cumsum(named.astype(jnp.int32)) - 1
    local_ids = jnp.arange(group_tiles, dtype=jnp.int32)
    picks = jnp.stack([jnp.sum(jnp.where(named & (rank == j), local_ids, 0)) for j in range(NEAR)])
    return (picks, rank)


def attend_tile(query_tile, key_values, key_live, feat_width):
    head_size = feat_width // HEADS
    key_rows = key_values.shape[0]
    queries_h = query_tile.reshape(TILE, HEADS, head_size)
    keys_h = key_values[:, :feat_width].reshape(key_rows, HEADS, head_size)
    values_h = key_values[:, feat_width:].reshape(key_rows, HEADS, head_size)
    scores = jnp.einsum(
        "qhd,khd->hqk", queries_h, keys_h, preferred_element_type=jnp.float32
    ) * head_size ** (-0.5)
    scores = jnp.where(key_live[None, None, :], scores, -jnp.inf)
    row_max = jnp.max(scores, axis=-1, keepdims=True)
    weights_raw = jnp.exp(scores - row_max)
    probs = (weights_raw / jnp.sum(weights_raw, axis=-1, keepdims=True)).astype(jnp.bfloat16)
    mixed_h = jnp.einsum("hqk,khd->qhd", probs, values_h, preferred_element_type=jnp.float32)
    return mixed_h.reshape(TILE, feat_width).astype(jnp.bfloat16)


def local(
    patches,
    vis_index,
    kv_list,
    kv_count,
    global_tiles,
    frame_table,
    space_table,
    ln_gain,
    ln_bias,
    w_qkv,
    w_out,
):
    tok_rows = patches.shape[0]
    feat_width = patches.shape[1]
    tile_count = tok_rows // TILE
    fsdp_size = lax.axis_size("fsdp")
    seq_size = lax.axis_size("seq")
    seq_at = lax.axis_index("seq")
    dev_at = seq_at * fsdp_size + lax.axis_index("fsdp")
    group_tiles = tile_count * fsdp_size
    stream = embed(patches, vis_index, frame_table, space_table)
    dev_count = seq_size * fsdp_size
    global_rows = []
    owners = []
    for slot_no in range(GLOBAL):
        tile_id = global_tiles[slot_no]
        owners.append(tile_id // tile_count)
        global_rows.append(lax.dynamic_slice_in_dim(stream, tile_id % tile_count * TILE, TILE, 0))
    global_stream = jnp.stack(global_rows)
    owners = jnp.stack(owners)
    bit_order = sorted(range(dev_count.bit_length() - 1), key=lambda b: -b)
    done_bits = 0
    for bit in bit_order:
        step = 1 << bit
        held = (dev_at ^ owners) & ~done_bits == 0
        got = lax.ppermute(
            global_stream, ("seq", "fsdp"), [(i, i ^ step) for i in range(dev_count)]
        )
        global_stream = jnp.where(held[:, None, None], global_stream, got)
        done_bits |= step
    global_stream = global_stream.reshape(GLOBAL * TILE, feat_width)
    w_full = lax.all_gather(w_qkv, "fsdp", axis=0, tiled=True)
    normed = layer_norm(stream, ln_gain, ln_bias)
    qkv = jnp.dot(normed, w_full, preferred_element_type=jnp.float32).astype(jnp.bfloat16)
    query = qkv[:, :feat_width]
    keyval = qkv[:, feat_width:]
    global_normed = layer_norm(global_stream, ln_gain, ln_bias)
    global_kv = (
        jnp.dot(global_normed, w_full[:, feat_width:], preferred_element_type=jnp.float32)
        .astype(jnp.bfloat16)
        .reshape(GLOBAL, TILE, 2 * feat_width)
    )
    group_block = lax.all_gather(keyval, "fsdp", axis=0, tiled=True).reshape(
        group_tiles, TILE, 2 * feat_width
    )
    near_blocks = []
    near_rank = []
    for reach in REACH:
        picks, rank = near_tiles(kv_list, seq_at + reach, group_tiles)
        asked = passed_along(picks, "seq", reach)
        near_blocks.append(passed_along(group_block[asked], "seq", -reach))
        near_rank.append(rank)
    window = jnp.concatenate([group_block] + near_blocks + [global_kv], axis=0)
    near_rank = jnp.stack(near_rank)
    entry_group = kv_list // group_tiles
    entry_local = kv_list % group_tiles
    reach_of = entry_group - seq_at
    reach_slot = jnp.where(reach_of < 0, reach_of + 2, reach_of + 1)
    reach_slot = jnp.clip(reach_slot, 0, len(REACH) - 1)
    entry_rank = near_rank[reach_slot, entry_local]
    local_lists = jnp.where(
        reach_of == 0, entry_local, group_tiles + NEAR * reach_slot + entry_rank
    )
    global_slots = group_tiles + NEAR * len(REACH) + jnp.arange(GLOBAL, dtype=jnp.int32)
    query_tiles = query.reshape(tile_count, TILE, feat_width)

    def per_tile(tile_args):
        query_tile, local_ids, live_count = tile_args
        slot_live_row = jnp.concatenate(
            [jnp.arange(KT) < live_count, jnp.ones((GLOBAL,), dtype=bool)]
        )
        key_live = jnp.repeat(slot_live_row, TILE)
        key_values = window[jnp.concatenate([local_ids, global_slots])].reshape(
            (KT + GLOBAL) * TILE, 2 * feat_width
        )
        return attend_tile(query_tile, key_values, key_live, feat_width)

    heads_out = lax.map(per_tile, (query_tiles, local_lists, kv_count)).reshape(
        tok_rows, feat_width
    )
    return jnp.dot(
        heads_out,
        lax.all_gather(w_out, "fsdp", axis=0, tiled=True),
        preferred_element_type=jnp.float32,
    ).astype(jnp.bfloat16)


def solution(mesh):
    return jax.shard_map(
        local,
        mesh=mesh,
        in_specs=(
            P(("seq", "fsdp"), None),
            P(("seq", "fsdp")),
            P(("seq", "fsdp"), None),
            P(("seq", "fsdp")),
            P(),
            P(),
            P(),
            P(),
            P(),
            P("fsdp", None),
            P("fsdp", None),
        ),
        out_specs=P(("seq", "fsdp"), None),
        check_vma=False,
    )
```

profile of v0, /device:TPU:88, one launch (start us, length us, event | category | flops | bytes accessed | tf_op | source)
XLA Modules:
  0.0 479.7 jit_solution(12287502584570003710)
XLA Ops:
  12.6 92.8 %all-gather.4.cloned.1.call-done = bf16[1280,3840]{1,0:T(8,128)(2,1)} async-done(((bf16[320,3840]{1,0:T(8,128)(2,1)}), bf16[1280,3840]{1,0:T(8,128)(2,1)}) %all-gather.4.cloned.1.call-update) | async-done | bytes 9830416 | tf_op jit(solution)/shard_map/all_gather | solution.py:108
  105.4 6.6 %convolution_convert_fusion = bf16[256,3840]{1,0:T(8,128)(2,1)S(1)} fusion(bf16[1280,3840]{1,0:T(8,128)(2,1)} %all-gather.4.cloned.1.call-done, bf16[256,1280]{1,0:T(8,128)(2,1)S(1)} %get-tuple-element.108, f32[1280]{0:T(1024)S(1)} %convert_element_type.133, f32[1280]{0:T(1024)S(1)} %convert_element_type.132, f32[256]{0:T(256)S(1)} %add_rsqrt_fusion, ...), kind=kOutput, calls=%fused_computation.34 | convolution fusion | flops 2519531520 | bytes 12464128 | tf_op jit(solution)/shard_map/dot_general | solution.py:110
  123.8 13.3 %collective-permute-done.8 = bf16[2,128,1280]{2,1,0:T(8,128)(2,1)S(1)} collective-permute-done((bf16[2,128,1280]{2,1,0:T(8,128)(2,1)S(1)}, bf16[2,128,1280]{2,1,0:T(8,128)(2,1)S(1)}, u32[]{:S(2)}, u32[]{:S(2)}) %collective-permute-start.8) | collective-permute-done | bytes 655392 | tf_op jit(solution)/shard_map/ppermute | solution.py:102
  139.3 13.6 %collective-permute-done.9 = bf16[2,128,1280]{2,1,0:T(8,128)(2,1)S(1)} collective-permute-done((bf16[2,128,1280]{2,1,0:T(8,128)(2,1)S(1)}, bf16[2,128,1280]{2,1,0:T(8,128)(2,1)S(1)}, u32[]{:S(2)}, u32[]{:S(2)}) %collective-permute-start.9) | collective-permute-done | bytes 655392 | tf_op jit(solution)/shard_map/ppermute | solution.py:102
  163.8 5.5 %collective-permute-done.10 = bf16[2,128,1280]{2,1,0:T(8,128)(2,1)S(1)} collective-permute-done((bf16[2,128,1280]{2,1,0:T(8,128)(2,1)S(1)}, bf16[2,128,1280]{2,1,0:T(8,128)(2,1)S(1)}, u32[]{:S(2)}, u32[]{:S(2)}) %collective-permute-start.10) | collective-permute-done | bytes 655392 | tf_op jit(solution)/shard_map/ppermute | solution.py:102
  175.3 8.0 %collective-permute-done.11 = bf16[2,128,1280]{2,1,0:T(8,128)(2,1)S(1)} collective-permute-done((bf16[2,128,1280]{2,1,0:T(8,128)(2,1)S(1)}, bf16[2,128,1280]{2,1,0:T(8,128)(2,1)S(1)}, u32[]{:S(2)}, u32[]{:S(2)}) %collective-permute-start.11) | collective-permute-done | bytes 655392 | tf_op jit(solution)/shard_map/ppermute | solution.py:102
  186.2 3.9 collective-permute-start.6
  192.1 23.7 %collective-permute-done.13 = bf16[2,128,1280]{2,1,0:T(8,128)(2,1)S(1)} collective-permute-done((bf16[2,128,1280]{2,1,0:T(8,128)(2,1)S(1)}, bf16[2,128,1280]{2,1,0:T(8,128)(2,1)S(1)}, u32[]{:S(2)}, u32[]{:S(2)}) %collective-permute-start.13) | collective-permute-done | bytes 655392 | tf_op jit(solution)/shard_map/ppermute | solution.py:102
  216.1 30.4 %collective-permute-done.14 = bf16[2,128,1280]{2,1,0:T(8,128)(2,1)S(1)} collective-permute-done((bf16[2,128,1280]{2,1,0:T(8,128)(2,1)S(1)}, bf16[2,128,1280]{2,1,0:T(8,128)(2,1)S(1)}, u32[]{:S(2)}, u32[]{:S(2)}) %collective-permute-start.14) | collective-permute-done | bytes 655392 | tf_op jit(solution)/shard_map/ppermute | solution.py:102
  246.9 4.5 gather_fusion.4
  254.1 4.5 gather_fusion.5
  260.5 4.6 gather_fusion.6
  269.1 4.7 gather_fusion.7
  273.8 4.0 collective-permute-start.7
  277.8 4.7 fusion.17
  282.8 16.5 %collective-permute-done.1 = bf16[3,128,2560]{2,1,0:T(8,128)(2,1)} collective-permute-done((bf16[3,128,2560]{2,1,0:T(8,128)(2,1)}, bf16[3,128,2560]{2,1,0:T(8,128)(2,1)}, u32[]{:S(2)}, u32[]{:S(2)}) %collective-permute-start.1) | collective-permute-done | bytes 1966112 | tf_op jit(solution)/shard_map/ppermute | solution.py:18
  301.0 15.2 %collective-permute-done.3 = bf16[3,128,2560]{2,1,0:T(8,128)(2,1)} collective-permute-done((bf16[3,128,2560]{2,1,0:T(8,128)(2,1)}, bf16[3,128,2560]{2,1,0:T(8,128)(2,1)}, u32[]{:S(2)}, u32[]{:S(2)}) %collective-permute-start.3) | collective-permute-done | bytes 1966112 | tf_op jit(solution)/shard_map/ppermute | solution.py:18
  319.7 17.5 %collective-permute-done.7 = bf16[3,128,2560]{2,1,0:T(8,128)(2,1)S(1)} collective-permute-done((bf16[3,128,2560]{2,1,0:T(8,128)(2,1)}, bf16[3,128,2560]{2,1,0:T(8,128)(2,1)S(1)}, u32[]{:S(2)}, u32[]{:S(2)}) %collective-permute-start.7) | collective-permute-done | bytes 1966112 | tf_op jit(solution)/shard_map/ppermute | solution.py:18
  337.5 5.0 %copy-done.2 = bf16[22,128,2560]{2,1,0:T(8,128)(2,1)} copy-done((bf16[22,128,2560]{2,1,0:T(8,128)(2,1)}, bf16[22,128,2560]{2,1,0:T(8,128)(2,1)S(1)}, u32[]{:S(2)}) %copy-start.2) | copy-done | bytes 14417944
  342.5 126.8 %while.11 = (s32[]{:T(128)}, bf16[2,128,1280]{2,1,0:T(8,128)(2,1)S(1)}, s32[2,16]{1,0:T(2,128)S(1)}, bf16[22,128,2560]{2,1,0:T(8,128)(2,1)}, s32[2]{0:T(128)S(1)...) while((s32[]{:T(128)}, bf16[2,128,1280]{2,1,0:T(8,128)(2,1)S(1)}, ...), condition=%wide.region_27.28_spmd.clone, body=%wide.region_24.27_spmd.clone.sunk | while | flops 1538428160 | bytes 123626584 | solution.py:154
  342.6 11.3 %gather_fusion = bf16[18,128,2560]{2,1,0:T(8,128)(2,1)} fusion(bf16[22,128,2560]{2,1,0:T(8,128)(2,1)} %get-tuple-element.203, s32[1024]{0:T(1024)S(1)} %pad_clamp_fusion.8), kind=kCustom, calls=%fused_computation.clone.clone.1 | custom fusion | bytes 23593032 | tf_op jit(solution)/shard_map/while/body/eval_jaxpr/gather | solution.py:149
  353.9 9.7 %fusion.97 = (bf16[2304,1280]{1,0:T(8,128)(2,1)}, bf16[2304,1280]{1,0:T(8,128)(2,1)}) fusion(bf16[2304,2560]{1,0:T(8,128)(2,1)} %bitcast.177), kind=kLoop, calls=%fused_computation.184.clone.1 | loop fusion | bytes 23592960 | tf_op jit(solution)/shard_map/while/body/eval_jaxpr/slice | solution.py:53
  363.5 8.9 %copy.34 = bf16[2304,1280]{0,1:T(8,128)(2,1)} copy(bf16[2304,1280]{1,0:T(8,128)(2,1)} %get-tuple-element.181) | data formatting | bytes 11796480 | tf_op jit(solution)/shard_map/while
  374.0 11.3 %fusion.98 = (f32[16,128]{1,0:T(8,128)S(1)}, f32[16,128,2304]{2,1,0:T(8,128)}) fusion(pred[2304]{0:T(1024)(128)(4,1)S(1)} %broadcast_bitcast_fusion.2, bf16[128,16,80]{0,2,1:T(8,128)(2,1)S(1)} %bitcast.187, bf16[2304,16,80]{0,2,1:T(8,128)(2,1)} %bitcast.178), kind=kOutput, calls=%fused_computation.185.clone.1 | convolution fusion | flops 773851392 | bytes 25110784 | tf_op jit(solution)/shard_map/while/body/eval_jaxpr/sub | solution.py:60
  385.3 8.9 %copy.32 = bf16[2304,1280]{0,1:T(8,128)(2,1)} copy(bf16[2304,1280]{1,0:T(8,128)(2,1)} %get-tuple-element.180) | data formatting | bytes 11796480 | tf_op jit(solution)/shard_map/while
  394.1 11.5 %fusion.99 = bf16[16,80,128]{2,1,0:T(8,128)(2,1)S(1)} fusion(bf16[2304,16,80]{0,2,1:T(8,128)(2,1)} %bitcast.179, f32[16,128,2304]{2,1,0:T(8,128)} %get-tuple-element.182, f32[16,128]{1,0:T(8,128)S(1)} %get-tuple-element.183), kind=kOutput, calls=%fused_computation.19.clone.1 | convolution fusion | flops 764575744 | bytes 25108480 | tf_op jit(solution)/shard_map/while/body/eval_jaxpr/hqk,khd->qhd/dot_general | solution.py:62
  406.0 11.3 %gather_fusion = bf16[18,128,2560]{2,1,0:T(8,128)(2,1)} fusion(bf16[22,128,2560]{2,1,0:T(8,128)(2,1)} %get-tuple-element.203, s32[1024]{0:T(1024)S(1)} %pad_clamp_fusion.8), kind=kCustom, calls=%fused_computation.clone.clone.1 | custom fusion | bytes 23593032 | tf_op jit(solution)/shard_map/while/body/eval_jaxpr/gather | solution.py:149
  417.3 9.7 %fusion.97 = (bf16[2304,1280]{1,0:T(8,128)(2,1)}, bf16[2304,1280]{1,0:T(8,128)(2,1)}) fusion(bf16[2304,2560]{1,0:T(8,128)(2,1)} %bitcast.177), kind=kLoop, calls=%fused_computation.184.clone.1 | loop fusion | bytes 23592960 | tf_op jit(solution)/shard_map/while/body/eval_jaxpr/slice | solution.py:53
  426.9 8.9 %copy.34 = bf16[2304,1280]{0,1:T(8,128)(2,1)} copy(bf16[2304,1280]{1,0:T(8,128)(2,1)} %get-tuple-element.181) | data formatting | bytes 11796480 | tf_op jit(solution)/shard_map/while
  437.4 11.3 %fusion.98 = (f32[16,128]{1,0:T(8,128)S(1)}, f32[16,128,2304]{2,1,0:T(8,128)}) fusion(pred[2304]{0:T(1024)(128)(4,1)S(1)} %broadcast_bitcast_fusion.2, bf16[128,16,80]{0,2,1:T(8,128)(2,1)S(1)} %bitcast.187, bf16[2304,16,80]{0,2,1:T(8,128)(2,1)} %bitcast.178), kind=kOutput, calls=%fused_computation.185.clone.1 | convolution fusion | flops 773851392 | bytes 25110784 | tf_op jit(solution)/shard_map/while/body/eval_jaxpr/sub | solution.py:60
  448.6 8.9 %copy.32 = bf16[2304,1280]{0,1:T(8,128)(2,1)} copy(bf16[2304,1280]{1,0:T(8,128)(2,1)} %get-tuple-element.180) | data formatting | bytes 11796480 | tf_op jit(solution)/shard_map/while
  457.5 11.5 %fusion.99 = bf16[16,80,128]{2,1,0:T(8,128)(2,1)S(1)} fusion(bf16[2304,16,80]{0,2,1:T(8,128)(2,1)} %bitcast.179, f32[16,128,2304]{2,1,0:T(8,128)} %get-tuple-element.182, f32[16,128]{1,0:T(8,128)S(1)} %get-tuple-element.183), kind=kOutput, calls=%fused_computation.19.clone.1 | convolution fusion | flops 764575744 | bytes 25108480 | tf_op jit(solution)/shard_map/while/body/eval_jaxpr/hqk,khd->qhd/dot_general | solution.py:62
  (148 shorter events, 58.6 us)
Async XLA Ops:
  6.5 4.1 copy-start
  6.5 2.8 copy-start.3
  6.5 98.9 %all-gather.4.cloned.1.call-start = ((), (), s32[]{:S(2)}) async-start(), calls=%async_computation | async-start | bytes 12288000 | tf_op jit(solution)/shard_map/all_gather | solution.py:108
  7.3 239.7 %all-gather.6.cloned.1.call-start = ((), (), s32[]{:S(2)}) async-start(), calls=%async_computation.1 | async-start | bytes 6553600 | tf_op jit(solution)/shard_map/all_gather | solution.py:119
  10.6 1.3 copy-start.5
  112.1 1.3 copy-start.4
  113.3 1.2 copy-start.7
  113.3 10.3 %copy-start.6 = (s32[2,16]{1,0:T(2,128)S(1)}, s32[2,16]{1,0:T(2,128)}, u32[]{:S(2)}) copy-start(s32[2,16]{1,0:T(2,128)} %param.15) | copy-start | bytes 388
  114.5 354.8 %all-gather.8.cloned.1.call-start = ((), (), s32[]{:S(2)}) async-start(), calls=%async_computation.2 | async-start | bytes 4096000 | tf_op jit(solution)/shard_map/all_gather | solution.py:159
  119.2 17.9 %collective-permute-start.8 = (bf16[2,128,1280]{2,1,0:T(8,128)(2,1)S(1)}, bf16[2,128,1280]{2,1,0:T(8,128)(2,1)S(1)}, u32[]{:S(2)}, u32[]{:S(2)}) collective-permute-start(bf16[2,128,1280]{2,1,0:T(8,128)(2,1)S(1)} %pad_maximum_fusion), channel_id=1, source_target_pairs={{0,64},{1,65},{2,66},{3,67},{4,68},{5,69},{6,70},{7,71},{8,72},{9,... | collective-permute-start | bytes 1966088 | tf_op jit(solution)/shard_map/ppermute | solution.py:102
  137.3 15.5 %collective-permute-start.9 = (bf16[2,128,1280]{2,1,0:T(8,128)(2,1)S(1)}, bf16[2,128,1280]{2,1,0:T(8,128)(2,1)S(1)}, u32[]{:S(2)}, u32[]{:S(2)}) collective-permute-start(bf16[2,128,1280]{2,1,0:T(8,128)(2,1)S(1)} %broadcast_select_fusion), channel_id=1, source_target_pairs={{0,32},{1,33},{2,34},{3,35},{4,36},{5,37},{6,38},{7,39},{8,40},{9,... | collective-permute-start | bytes 1966088 | tf_op jit(solution)/shard_map/ppermute | solution.py:102
  153.0 16.3 %collective-permute-start.10 = (bf16[2,128,1280]{2,1,0:T(8,128)(2,1)S(1)}, bf16[2,128,1280]{2,1,0:T(8,128)(2,1)S(1)}, u32[]{:S(2)}, u32[]{:S(2)}) collective-permute-start(bf16[2,128,1280]{2,1,0:T(8,128)(2,1)S(1)} %broadcast_select_fusion.1), channel_id=1, source_target_pairs={{0,16},{1,17},{2,18},{3,19},{4,20},{5,21},{6,22},{7,23},{8,24},{9,... | collective-permute-start | bytes 1966088 | tf_op jit(solution)/shard_map/ppermute | solution.py:102
  157.1 34.9 %collective-permute-start = (s32[3]{0:T(128)S(1)}, s32[3]{0:T(128)S(1)}, u32[]{:S(2)}, u32[]{:S(2)}) collective-permute-start(s32[3]{0:T(128)S(1)} %pad_add_fusion.1), channel_id=1, source_target_pairs={{8,0},{12,4},{16,8},{20,12},{24,16},{28,20},{32,24},{36,28},{40,32... | collective-permute-start | bytes 44 | tf_op jit(solution)/shard_map/ppermute | solution.py:18
  161.9 30.1 %collective-permute-start.2 = (s32[3]{0:T(128)S(1)}, s32[3]{0:T(128)S(1)}, u32[]{:S(2)}, u32[]{:S(2)}) collective-permute-start(s32[3]{0:T(128)S(1)} %pad_add_fusion.2), channel_id=1, source_target_pairs={{4,0},{8,4},{12,8},{16,12},{20,16},{24,20},{28,24},{32,28},{36,32}... | collective-permute-start | bytes 44 | tf_op jit(solution)/shard_map/ppermute | solution.py:18
  169.4 13.9 %collective-permute-start.11 = (bf16[2,128,1280]{2,1,0:T(8,128)(2,1)S(1)}, bf16[2,128,1280]{2,1,0:T(8,128)(2,1)S(1)}, u32[]{:S(2)}, u32[]{:S(2)}) collective-permute-start(bf16[2,128,1280]{2,1,0:T(8,128)(2,1)S(1)} %broadcast_select_fusion.2), channel_id=1, source_target_pairs={{0,8},{1,9},{2,10},{3,11},{4,12},{5,13},{6,14},{7,15},{8,0},{9,1},... | collective-permute-start | bytes 1966088 | tf_op jit(solution)/shard_map/ppermute | solution.py:102
  173.2 42.9 %collective-permute-start.4 = (s32[3]{0:T(128)S(1)}, s32[3]{0:T(128)S(1)}, u32[]{:S(2)}, u32[]{:S(2)}) collective-permute-start(s32[3]{0:T(128)S(1)} %pad_add_fusion.3), channel_id=1, source_target_pairs={{0,4},{4,8},{8,12},{12,16},{16,20},{20,24},{24,28},{28,32},{32,36}... | collective-permute-start | bytes 44 | tf_op jit(solution)/shard_map/ppermute | solution.py:18
  183.4 6.7 %collective-permute-start.12 = (bf16[2,128,1280]{2,1,0:T(8,128)(2,1)S(1)}, bf16[2,128,1280]{2,1,0:T(8,128)(2,1)S(1)}, u32[]{:S(2)}, u32[]{:S(2)}) collective-permute-start(bf16[2,128,1280]{2,1,0:T(8,128)(2,1)S(1)} %broadcast_select_fusion.3), channel_id=1, source_target_pairs={{0,4},{1,5},{2,6},{3,7},{4,0},{5,1},{6,2},{7,3},{8,12},{9,13},{10,... | collective-permute-start | bytes 1966088 | tf_op jit(solution)/shard_map/ppermute | solution.py:102
  186.2 29.9 %collective-permute-start.6 = (s32[3]{0:T(128)S(1)}, s32[3]{0:T(128)S(1)}, u32[]{:S(2)}, u32[]{:S(2)}) collective-permute-start(s32[3]{0:T(128)S(1)} %pad_add_fusion.4), channel_id=1, source_target_pairs={{0,8},{4,12},{8,16},{12,20},{16,24},{20,28},{24,32},{28,36},{32,40... | collective-permute-start | bytes 44 | tf_op jit(solution)/shard_map/ppermute | solution.py:18
  190.3 25.5 %collective-permute-start.13 = (bf16[2,128,1280]{2,1,0:T(8,128)(2,1)S(1)}, bf16[2,128,1280]{2,1,0:T(8,128)(2,1)S(1)}, u32[]{:S(2)}, u32[]{:S(2)}) collective-permute-start(bf16[2,128,1280]{2,1,0:T(8,128)(2,1)S(1)} %broadcast_select_fusion.4), channel_id=1, source_target_pairs={{0,2},{1,3},{2,0},{3,1},{4,6},{5,7},{6,4},{7,5},{8,10},{9,11},{10,... | collective-permute-start | bytes 1966088 | tf_op jit(solution)/shard_map/ppermute | solution.py:102
  216.0 30.6 %collective-permute-start.14 = (bf16[2,128,1280]{2,1,0:T(8,128)(2,1)S(1)}, bf16[2,128,1280]{2,1,0:T(8,128)(2,1)S(1)}, u32[]{:S(2)}, u32[]{:S(2)}) collective-permute-start(bf16[2,128,1280]{2,1,0:T(8,128)(2,1)S(1)} %broadcast_select_fusion.5), channel_id=1, source_target_pairs={{0,1},{1,0},{2,3},{3,2},{4,5},{5,4},{6,7},{7,6},{8,9},{9,8},{10,11... | collective-permute-start | bytes 1966088 | tf_op jit(solution)/shard_map/ppermute | solution.py:102
  251.5 47.9 %collective-permute-start.1 = (bf16[3,128,2560]{2,1,0:T(8,128)(2,1)}, bf16[3,128,2560]{2,1,0:T(8,128)(2,1)}, u32[]{:S(2)}, u32[]{:S(2)}) collective-permute-start(bf16[3,128,2560]{2,1,0:T(8,128)(2,1)} %gather_fusion.4), channel_id=1, source_target_pairs={{0,8},{4,12},{8,16},{12,20},{16,24},{20,28},{24,32},{28,36},{32,40... | collective-permute-start | bytes 5898248 | tf_op jit(solution)/shard_map/ppermute | solution.py:18
  258.6 57.7 %collective-permute-start.3 = (bf16[3,128,2560]{2,1,0:T(8,128)(2,1)}, bf16[3,128,2560]{2,1,0:T(8,128)(2,1)}, u32[]{:S(2)}, u32[]{:S(2)}) collective-permute-start(bf16[3,128,2560]{2,1,0:T(8,128)(2,1)} %gather_fusion.5), channel_id=1, source_target_pairs={{0,4},{4,8},{8,12},{12,16},{16,20},{20,24},{24,28},{28,32},{32,36}... | collective-permute-start | bytes 5898248 | tf_op jit(solution)/shard_map/ppermute | solution.py:18
  265.1 52.9 %collective-permute-start.5 = (bf16[3,128,2560]{2,1,0:T(8,128)(2,1)}, bf16[3,128,2560]{2,1,0:T(8,128)(2,1)}, u32[]{:S(2)}, u32[]{:S(2)}) collective-permute-start(bf16[3,128,2560]{2,1,0:T(8,128)(2,1)} %gather_fusion.6), channel_id=1, source_target_pairs={{4,0},{8,4},{12,8},{16,12},{20,16},{24,20},{28,24},{32,28},{36,32}... | collective-permute-start | bytes 5898248 | tf_op jit(solution)/shard_map/ppermute | solution.py:18
  269.1 13.4 %slice-start = ((s8[5242880]{0:T(1024)(128)(4,1)}), s8[1048576]{0:T(1024)(128)(4,1)S(1)}, s32[]{:S(2)}) async-start(s8[5242880]{0:T(1024)(128)(4,1)} %bitcast.184), calls=%async_computation.3 | async-start | bytes 2097152
  273.7 8.7 %slice-start.1 = ((s8[5242880]{0:T(1024)(128)(4,1)}), s8[4194304]{0:T(1024)(128)(4,1)S(1)}, s32[]{:S(2)}) async-start(s8[5242880]{0:T(1024)(128)(4,1)} %bitcast.184), calls=%async_computation.4 | async-start | bytes 8388608
  273.8 63.5 %collective-permute-start.7 = (bf16[3,128,2560]{2,1,0:T(8,128)(2,1)}, bf16[3,128,2560]{2,1,0:T(8,128)(2,1)S(1)}, u32[]{:S(2)}, u32[]{:S(2)}) collective-permute-start(bf16[3,128,2560]{2,1,0:T(8,128)(2,1)} %gather_fusion.7), channel_id=1, source_target_pairs={{8,0},{12,4},{16,8},{20,12},{24,16},{28,20},{32,24},{36,28},{40,32... | collective-permute-start | bytes 5898248 | tf_op jit(solution)/shard_map/ppermute | solution.py:18
  319.6 22.9 %slice-start.2 = ((bf16[256,3840]{1,0:T(8,128)(2,1)}), bf16[256,1280]{1,0:T(8,128)(2,1)S(1)}, s32[]{:S(2)}) async-start(bf16[256,3840]{1,0:T(8,128)(2,1)} %copy-done.4), calls=%async_computation.5 | async-start | bytes 1310720 | tf_op jit(solution)/shard_map/slice | solution.py:111
  319.6 22.9 %copy-start.8 = (bf16[2,128,1280]{2,1,0:T(8,128)(2,1)S(1)}, bf16[2,128,1280]{2,1,0:T(8,128)(2,1)}, u32[]{:S(2)}) copy-start(bf16[2,128,1280]{2,1,0:T(8,128)(2,1)} %custom-call.17) | copy-start | bytes 1966084
  319.6 22.9 %copy-start.9 = (s32[2]{0:T(128)S(1)}, s32[2]{0:T(128)}, u32[]{:S(2)}) copy-start(s32[2]{0:T(128)} %param.16) | copy-start | bytes 28
  337.5 5.0 %copy-start.2 = (bf16[22,128,2560]{2,1,0:T(8,128)(2,1)}, bf16[22,128,2560]{2,1,0:T(8,128)(2,1)S(1)}, u32[]{:S(2)}) copy-start(bf16[22,128,2560]{2,1,0:T(8,128)(2,1)S(1)} %constant_dynamic-update-slice_fusion.1) | copy-start | bytes 43253764
  469.3 3.9 copy-start.1
Sparse Core Ops, SparseCore 0:
  9.0 96.3 all-gather.3
  114.6 57.4 all-gather.5
  190.3 58.4 all-gather.7
where the time goes:
time: 481 us; the launch traced here: 480 us
  waiting for transfers between devices  237 us (49%)
  local copies, waits for them, and re-layouts  115 us (24%)
  matrix products  60.9 us (13%)
  starting transfers between devices  29.4 us (6%)
  between operations  18.8 us (4%)
  other arithmetic  17.9 us (4%)
    ppermute x7, waiting for transfers between devices, local(): lax.ppermute(global_stream, ('seq', 'fsdp'), [(i, i ^ step) for i in rang...  94.5 us
    all_gather x1, waiting for transfers between devices, local(): w_full = lax.all_gather(w_qkv, 'fsdp', axis=0, tiled=True)  92.8 us
    ppermute x8, waiting for transfers between devices, passed_along(): return lax.ppermute(block, axis, route)  49.3 us
    while x4, local copies, waits for them, and re-layouts  35.4 us
    dot_general x2, matrix products, attend_tile(): jnp.einsum('hqk,khd->qhd', probs, values_h, preferred_element_type=jnp.fl...  23.1 us
    sub x2, matrix products, attend_tile(): weights_raw = jnp.exp(scores - row_max)  22.6 us
    gather x2, local copies, waits for them, and re-layouts, per_tile(): window[jnp.concatenate([local_ids, global_slots])]  22.5 us
    ppermute x8, starting transfers between devices, passed_along(): return lax.ppermute(block, axis, route)  21.4 us
  transfers between devices with their start and end apart: 18, of which 10 were waited for; matrix products, arithmetic and copies ran while one was open for 37% of the time, Pallas kernels for 0%

commit v1 on v0

--- a/solution.py
+++ b/solution.py
@@ -105,7 +105,9 @@
         global_stream = jnp.where(held[:, None, None], global_stream, got)
         done_bits |= step
     global_stream = global_stream.reshape(GLOBAL * TILE, feat_width)
-    w_full = lax.all_gather(w_qkv, "fsdp", axis=0, tiled=True)
+    w_full = jnp.concatenate(
+        lax.all_to_all(jnp.stack([w_qkv] * lax.axis_size("fsdp")), "fsdp", 0, 0), axis=0
+    )
     normed = layer_norm(stream, ln_gain, ln_bias)
     qkv = jnp.dot(normed, w_full, preferred_element_type=jnp.float32).astype(jnp.bfloat16)
     query = qkv[:, :feat_width]

time: 481 us -> 502 us (1.044)
  starting transfers between devices: 29.4 us -> 42.3 us
  local copies, waits for them, and re-layouts: 115 us -> 121 us
    all_to_all x0 -> x1, waiting for transfers between devices: none -> 103 us  [local(): lax.all_to_all(jnp.stack([w_qkv] * lax.axis_size('fsdp')), 'fsdp', 0, 0)]
    all_gather x1 -> x0, waiting for transfers between devices: 92.8 us -> none  [local(): w_full = lax.all_gather(w_qkv, 'fsdp', axis=0, tiled=True)]
    ppermute x7, waiting for transfers between devices: 94.5 us -> 85.7 us  [local(): lax.ppermute(global_stream, ('seq', 'fsdp'), [(i, i ^ step) for i in rang...]
    another operation x0 -> x1, local copies, waits for them, and re-layouts: none -> 6.2 us  [local(): jnp.stack([w_qkv] * lax.axis_size('fsdp'))]
    all_to_all x0 -> x1, starting transfers between devices: none -> 6.04 us  [local(): lax.all_to_all(jnp.stack([w_qkv] * lax.axis_size('fsdp')), 'fsdp', 0, 0)]
    unnamed x29 -> x35, local copies, waits for them, and re-layouts: 11.8 us -> 11.8 us
  transfers between devices with their start and end apart: 18 -> 18, of which waited for: 10 -> 10; matrix products, arithmetic and copies ran while one was open for 37% -> 35% of each run, Pallas kernels for 0% -> 0%
where the time goes in v1:
time: 502 us; the launch traced here: 497 us
  waiting for transfers between devices  237 us (47%)
  local copies, waits for them, and re-layouts  121 us (24%)
  matrix products  60.9 us (12%)
  starting transfers between devices  42.3 us (8%)
  between operations  19.2 us (4%)
  other arithmetic  15.9 us (3%)
    all_to_all x1, waiting for transfers between devices, local(): lax.all_to_all(jnp.stack([w_qkv] * lax.axis_size('fsdp')), 'fsdp', 0, 0)  103 us
    ppermute x7, waiting for transfers between devices, local(): lax.ppermute(global_stream, ('seq', 'fsdp'), [(i, i ^ step) for i in rang...  85.7 us
    ppermute x8, waiting for transfers between devices, passed_along(): return lax.ppermute(block, axis, route)  48.3 us
    while x4, local copies, waits for them, and re-layouts  35.4 us
    ppermute x8, starting transfers between devices, passed_along(): return lax.ppermute(block, axis, route)  23.4 us
    dot_general x2, matrix products, attend_tile(): jnp.einsum('hqk,khd->qhd', probs, values_h, preferred_element_type=jnp.fl...  23.1 us
    sub x2, matrix products, attend_tile(): weights_raw = jnp.exp(scores - row_max)  22.6 us
    gather x2, local copies, waits for them, and re-layouts, per_tile(): window[jnp.concatenate([local_ids, global_slots])]  22.5 us
  transfers between devices with their start and end apart: 18, of which 10 were waited for; matrix products, arithmetic and copies ran while one was open for 35% of the time, Pallas kernels for 0%

profile of v1, /device:TPU:88, one launch (start us, length us, event | category | flops | bytes accessed | tf_op | source)
XLA Modules:
  0.0 496.7 jit_solution(8497161101955536673)
XLA Ops:
  6.5 6.2 %stack.81 = bf16[4,320,3840]{2,1,0:T(8,128)(2,1)} broadcast(bf16[320,3840]{1,0:T(8,128)(2,1)} %param.22), dimensions={1,2} | broadcast | bytes 12288000 | tf_op jit(solution)/shard_map/stack | solution.py:109
  12.7 6.0 %all-to-all-start = ((bf16[4,320,3840]{2,1,0:T(8,128)(2,1)}), bf16[4,320,3840]{2,1,0:T(8,128)(2,1)}, u32[]{:S(2)}, u32[]{:S(2)}) async-start(bf16[4,320,3840]{2,1,0:T(8,128)(2,1)} %stack.81), calls=%async_computation | async-start | bytes 19660800 | tf_op jit(solution)/shard_map/all_to_all | solution.py:109
  22.2 103.0 %all-to-all-done = bf16[4,320,3840]{2,1,0:T(8,128)(2,1)} async-done(((bf16[4,320,3840]{2,1,0:T(8,128)(2,1)}), bf16[4,320,3840]{2,1,0:T(8,128)(2,1)}, u32[]{:S(2)}, u32[]{:S(2)}) %all-to-all-start) | async-done | bytes 9830432 | tf_op jit(solution)/shard_map/all_to_all | solution.py:109
  125.2 6.6 %convolution_convert_fusion = bf16[256,3840]{1,0:T(8,128)(2,1)S(1)} fusion(bf16[1280,3840]{1,0:T(8,128)(2,1)} %bitcast.8, bf16[256,1280]{1,0:T(8,128)(2,1)S(1)} %get-tuple-element.108, f32[1280]{0:T(1024)S(1)} %convert_element_type.133, f32[1280]{0:T(1024)S(1)} %convert_element_type.132, f32[256]{0:T(256)S(1)} %add_rsqrt_fusion, ...), kind=kOutput, calls=%fused_computation.34 | convolution fusion | flops 2519531520 | bytes 12464128 | tf_op jit(solution)/shard_map/dot_general | solution.py:112
  143.6 12.5 %collective-permute-done.8 = bf16[2,128,1280]{2,1,0:T(8,128)(2,1)S(1)} collective-permute-done((bf16[2,128,1280]{2,1,0:T(8,128)(2,1)S(1)}, bf16[2,128,1280]{2,1,0:T(8,128)(2,1)S(1)}, u32[]{:S(2)}, u32[]{:S(2)}) %collective-permute-start.8) | collective-permute-done | bytes 655392 | tf_op jit(solution)/shard_map/ppermute | solution.py:102
  158.2 12.7 %collective-permute-done.9 = bf16[2,128,1280]{2,1,0:T(8,128)(2,1)S(1)} collective-permute-done((bf16[2,128,1280]{2,1,0:T(8,128)(2,1)S(1)}, bf16[2,128,1280]{2,1,0:T(8,128)(2,1)S(1)}, u32[]{:S(2)}, u32[]{:S(2)}) %collective-permute-start.9) | collective-permute-done | bytes 655392 | tf_op jit(solution)/shard_map/ppermute | solution.py:102
  192.5 7.3 %collective-permute-done.11 = bf16[2,128,1280]{2,1,0:T(8,128)(2,1)S(1)} collective-permute-done((bf16[2,128,1280]{2,1,0:T(8,128)(2,1)S(1)}, bf16[2,128,1280]{2,1,0:T(8,128)(2,1)S(1)}, u32[]{:S(2)}, u32[]{:S(2)}) %collective-permute-start.11) | collective-permute-done | bytes 655392 | tf_op jit(solution)/shard_map/ppermute | solution.py:102
  202.8 5.3 %collective-permute-start.6 = (s32[3]{0:T(128)S(1)}, s32[3]{0:T(128)S(1)}, u32[]{:S(2)}, u32[]{:S(2)}) collective-permute-start(s32[3]{0:T(128)S(1)} %pad_add_fusion.4), channel_id=1, source_target_pairs={{0,8},{4,12},{8,16},{12,20},{16,24},{20,28},{24,32},{28,36},{32,40... | collective-permute-start | bytes 44 | tf_op jit(solution)/shard_map/ppermute | solution.py:18
  213.5 19.6 %collective-permute-done.13 = bf16[2,128,1280]{2,1,0:T(8,128)(2,1)S(1)} collective-permute-done((bf16[2,128,1280]{2,1,0:T(8,128)(2,1)S(1)}, bf16[2,128,1280]{2,1,0:T(8,128)(2,1)S(1)}, u32[]{:S(2)}, u32[]{:S(2)}) %collective-permute-start.13) | collective-permute-done | bytes 655392 | tf_op jit(solution)/shard_map/ppermute | solution.py:102
  234.9 29.4 %collective-permute-done.14 = bf16[2,128,1280]{2,1,0:T(8,128)(2,1)S(1)} collective-permute-done((bf16[2,128,1280]{2,1,0:T(8,128)(2,1)S(1)}, bf16[2,128,1280]{2,1,0:T(8,128)(2,1)S(1)}, u32[]{:S(2)}, u32[]{:S(2)}) %collective-permute-start.14) | collective-permute-done | bytes 655392 | tf_op jit(solution)/shard_map/ppermute | solution.py:102
  264.6 4.5 gather_fusion.4
  272.2 4.5 gather_fusion.5
  278.6 4.6 gather_fusion.6
  287.3 4.7 gather_fusion.7
  295.4 4.7 fusion.17
  300.5 16.5 %collective-permute-done.1 = bf16[3,128,2560]{2,1,0:T(8,128)(2,1)} collective-permute-done((bf16[3,128,2560]{2,1,0:T(8,128)(2,1)}, bf16[3,128,2560]{2,1,0:T(8,128)(2,1)}, u32[]{:S(2)}, u32[]{:S(2)}) %collective-permute-start.1) | collective-permute-done | bytes 1966112 | tf_op jit(solution)/shard_map/ppermute | solution.py:18
  318.7 16.5 %collective-permute-done.3 = bf16[3,128,2560]{2,1,0:T(8,128)(2,1)} collective-permute-done((bf16[3,128,2560]{2,1,0:T(8,128)(2,1)}, bf16[3,128,2560]{2,1,0:T(8,128)(2,1)}, u32[]{:S(2)}, u32[]{:S(2)}) %collective-permute-start.3) | collective-permute-done | bytes 1966112 | tf_op jit(solution)/shard_map/ppermute | solution.py:18
  338.6 15.3 %collective-permute-done.7 = bf16[3,128,2560]{2,1,0:T(8,128)(2,1)S(1)} collective-permute-done((bf16[3,128,2560]{2,1,0:T(8,128)(2,1)}, bf16[3,128,2560]{2,1,0:T(8,128)(2,1)S(1)}, u32[]{:S(2)}, u32[]{:S(2)}) %collective-permute-start.7) | collective-permute-done | bytes 1966112 | tf_op jit(solution)/shard_map/ppermute | solution.py:18
  354.1 5.0 %copy-done.2 = bf16[22,128,2560]{2,1,0:T(8,128)(2,1)} copy-done((bf16[22,128,2560]{2,1,0:T(8,128)(2,1)}, bf16[22,128,2560]{2,1,0:T(8,128)(2,1)S(1)}, u32[]{:S(2)}) %copy-start.2) | copy-done | bytes 14417944
  359.2 126.8 %while.11 = (s32[]{:T(128)}, bf16[2,128,1280]{2,1,0:T(8,128)(2,1)S(1)}, s32[2,16]{1,0:T(2,128)S(1)}, bf16[22,128,2560]{2,1,0:T(8,128)(2,1)}, s32[2]{0:T(128)S(1)...) while((s32[]{:T(128)}, bf16[2,128,1280]{2,1,0:T(8,128)(2,1)S(1)}, ...), condition=%wide.region_27.28_spmd.clone, body=%wide.region_24.27_spmd.clone.sunk | while | flops 1538428160 | bytes 123626584 | solution.py:156
  359.3 11.3 %gather_fusion = bf16[18,128,2560]{2,1,0:T(8,128)(2,1)} fusion(bf16[22,128,2560]{2,1,0:T(8,128)(2,1)} %get-tuple-element.203, s32[1024]{0:T(1024)S(1)} %pad_clamp_fusion.8), kind=kCustom, calls=%fused_computation.clone.clone.1 | custom fusion | bytes 23593032 | tf_op jit(solution)/shard_map/while/body/eval_jaxpr/gather | solution.py:151
  370.6 9.7 %fusion.97 = (bf16[2304,1280]{1,0:T(8,128)(2,1)}, bf16[2304,1280]{1,0:T(8,128)(2,1)}) fusion(bf16[2304,2560]{1,0:T(8,128)(2,1)} %bitcast.178), kind=kLoop, calls=%fused_computation.184.clone.1 | loop fusion | bytes 23592960 | tf_op jit(solution)/shard_map/while/body/eval_jaxpr/slice | solution.py:53
  380.2 8.9 %copy.34 = bf16[2304,1280]{0,1:T(8,128)(2,1)} copy(bf16[2304,1280]{1,0:T(8,128)(2,1)} %get-tuple-element.181) | data formatting | bytes 11796480 | tf_op jit(solution)/shard_map/while
  390.6 11.3 %fusion.98 = (f32[16,128]{1,0:T(8,128)S(1)}, f32[16,128,2304]{2,1,0:T(8,128)}) fusion(pred[2304]{0:T(1024)(128)(4,1)S(1)} %broadcast_bitcast_fusion.2, bf16[128,16,80]{0,2,1:T(8,128)(2,1)S(1)} %bitcast.188, bf16[2304,16,80]{0,2,1:T(8,128)(2,1)} %bitcast.179), kind=kOutput, calls=%fused_computation.185.clone.1 | convolution fusion | flops 773851392 | bytes 25110784 | tf_op jit(solution)/shard_map/while/body/eval_jaxpr/sub | solution.py:60
  401.9 8.9 %copy.32 = bf16[2304,1280]{0,1:T(8,128)(2,1)} copy(bf16[2304,1280]{1,0:T(8,128)(2,1)} %get-tuple-element.180) | data formatting | bytes 11796480 | tf_op jit(solution)/shard_map/while
  410.8 11.5 %fusion.99 = bf16[16,80,128]{2,1,0:T(8,128)(2,1)S(1)} fusion(bf16[2304,16,80]{0,2,1:T(8,128)(2,1)} %bitcast.180, f32[16,128,2304]{2,1,0:T(8,128)} %get-tuple-element.182, f32[16,128]{1,0:T(8,128)S(1)} %get-tuple-element.183), kind=kOutput, calls=%fused_computation.19.clone.1 | convolution fusion | flops 764575744 | bytes 25108480 | tf_op jit(solution)/shard_map/while/body/eval_jaxpr/hqk,khd->qhd/dot_general | solution.py:62
  422.7 11.3 %gather_fusion = bf16[18,128,2560]{2,1,0:T(8,128)(2,1)} fusion(bf16[22,128,2560]{2,1,0:T(8,128)(2,1)} %get-tuple-element.203, s32[1024]{0:T(1024)S(1)} %pad_clamp_fusion.8), kind=kCustom, calls=%fused_computation.clone.clone.1 | custom fusion | bytes 23593032 | tf_op jit(solution)/shard_map/while/body/eval_jaxpr/gather | solution.py:151
  433.9 9.7 %fusion.97 = (bf16[2304,1280]{1,0:T(8,128)(2,1)}, bf16[2304,1280]{1,0:T(8,128)(2,1)}) fusion(bf16[2304,2560]{1,0:T(8,128)(2,1)} %bitcast.178), kind=kLoop, calls=%fused_computation.184.clone.1 | loop fusion | bytes 23592960 | tf_op jit(solution)/shard_map/while/body/eval_jaxpr/slice | solution.py:53
  443.6 8.9 %copy.34 = bf16[2304,1280]{0,1:T(8,128)(2,1)} copy(bf16[2304,1280]{1,0:T(8,128)(2,1)} %get-tuple-element.181) | data formatting | bytes 11796480 | tf_op jit(solution)/shard_map/while
  454.0 11.3 %fusion.98 = (f32[16,128]{1,0:T(8,128)S(1)}, f32[16,128,2304]{2,1,0:T(8,128)}) fusion(pred[2304]{0:T(1024)(128)(4,1)S(1)} %broadcast_bitcast_fusion.2, bf16[128,16,80]{0,2,1:T(8,128)(2,1)S(1)} %bitcast.188, bf16[2304,16,80]{0,2,1:T(8,128)(2,1)} %bitcast.179), kind=kOutput, calls=%fused_computation.185.clone.1 | convolution fusion | flops 773851392 | bytes 25110784 | tf_op jit(solution)/shard_map/while/body/eval_jaxpr/sub | solution.py:60
  465.3 8.9 %copy.32 = bf16[2304,1280]{0,1:T(8,128)(2,1)} copy(bf16[2304,1280]{1,0:T(8,128)(2,1)} %get-tuple-element.180) | data formatting | bytes 11796480 | tf_op jit(solution)/shard_map/while
  474.2 11.5 %fusion.99 = bf16[16,80,128]{2,1,0:T(8,128)(2,1)S(1)} fusion(bf16[2304,16,80]{0,2,1:T(8,128)(2,1)} %bitcast.180, f32[16,128,2304]{2,1,0:T(8,128)} %get-tuple-element.182, f32[16,128]{1,0:T(8,128)S(1)} %get-tuple-element.183), kind=kOutput, calls=%fused_computation.19.clone.1 | convolution fusion | flops 764575744 | bytes 25108480 | tf_op jit(solution)/shard_map/while/body/eval_jaxpr/hqk,khd->qhd/dot_general | solution.py:62
  (154 shorter events, 69.5 us)
Async XLA Ops:
  6.5 13.7 %copy-start = (bf16[512,1280]{1,0:T(8,128)(2,1)S(1)}, bf16[512,1280]{1,0:T(8,128)(2,1)}, u32[]{:S(2)}) copy-start(bf16[512,1280]{1,0:T(8,128)(2,1)} %param.19) | copy-start | bytes 3932164
  12.7 6.1 %copy-start.6 = (bf16[1280]{0:T(1024)(128)(2,1)S(1)}, bf16[1280]{0:T(1024)(128)(2,1)}, u32[]{:S(2)}) copy-start(bf16[1280]{0:T(1024)(128)(2,1)} %param.20) | copy-start | bytes 7684
  12.7 6.1 %copy-start.7 = (bf16[1280]{0:T(1024)(128)(2,1)S(1)}, bf16[1280]{0:T(1024)(128)(2,1)}, u32[]{:S(2)}) copy-start(bf16[1280]{0:T(1024)(128)(2,1)} %param.21) | copy-start | bytes 7684
  12.7 6.1 %copy-start.10 = (s32[256]{0:T(256)S(1)}, s32[256]{0:T(256)}, u32[]{:S(2)}) copy-start(s32[256]{0:T(256)} %param.14) | copy-start | bytes 3076
  12.7 6.2 %copy-start.3 = (bf16[256,1280]{1,0:T(8,128)(2,1)S(1)}, bf16[256,1280]{1,0:T(8,128)(2,1)}, u32[]{:S(2)}) copy-start(bf16[256,1280]{1,0:T(8,128)(2,1)} %param.18) | copy-start | bytes 1966084
  12.7 112.4 %all-to-all-start = ((bf16[4,320,3840]{2,1,0:T(8,128)(2,1)}), bf16[4,320,3840]{2,1,0:T(8,128)(2,1)}, u32[]{:S(2)}, u32[]{:S(2)}) async-start(bf16[4,320,3840]{2,1,0:T(8,128)(2,1)} %stack.81), calls=%async_computation | async-start | bytes 19660800 | tf_op jit(solution)/shard_map/all_to_all | solution.py:109
  18.8 245.8 %all-gather.3.cloned.1.call-start = ((), (), s32[]{:S(2)}) async-start(), calls=%async_computation.1 | async-start | bytes 6553600 | tf_op jit(solution)/shard_map/all_gather | solution.py:121
  20.2 1.3 copy-start.5
  133.1 10.3 %copy-start.8 = (s32[2,16]{1,0:T(2,128)S(1)}, s32[2,16]{1,0:T(2,128)}, u32[]{:S(2)}) copy-start(s32[2,16]{1,0:T(2,128)} %param.15) | copy-start | bytes 388
  134.2 351.7 %all-gather.5.cloned.1.call-start = ((), (), s32[]{:S(2)}) async-start(), calls=%async_computation.2 | async-start | bytes 4096000 | tf_op jit(solution)/shard_map/all_gather | solution.py:161
  139.0 17.1 %collective-permute-start.8 = (bf16[2,128,1280]{2,1,0:T(8,128)(2,1)S(1)}, bf16[2,128,1280]{2,1,0:T(8,128)(2,1)S(1)}, u32[]{:S(2)}, u32[]{:S(2)}) collective-permute-start(bf16[2,128,1280]{2,1,0:T(8,128)(2,1)S(1)} %pad_maximum_fusion), channel_id=1, source_target_pairs={{0,64},{1,65},{2,66},{3,67},{4,68},{5,69},{6,70},{7,71},{8,72},{9,... | collective-permute-start | bytes 1966088 | tf_op jit(solution)/shard_map/ppermute | solution.py:102
  156.2 14.7 %collective-permute-start.9 = (bf16[2,128,1280]{2,1,0:T(8,128)(2,1)S(1)}, bf16[2,128,1280]{2,1,0:T(8,128)(2,1)S(1)}, u32[]{:S(2)}, u32[]{:S(2)}) collective-permute-start(bf16[2,128,1280]{2,1,0:T(8,128)(2,1)S(1)} %broadcast_select_fusion), channel_id=1, source_target_pairs={{0,32},{1,33},{2,34},{3,35},{4,36},{5,37},{6,38},{7,39},{8,40},{9,... | collective-permute-start | bytes 1966088 | tf_op jit(solution)/shard_map/ppermute | solution.py:102
  171.1 15.5 %collective-permute-start.10 = (bf16[2,128,1280]{2,1,0:T(8,128)(2,1)S(1)}, bf16[2,128,1280]{2,1,0:T(8,128)(2,1)S(1)}, u32[]{:S(2)}, u32[]{:S(2)}) collective-permute-start(bf16[2,128,1280]{2,1,0:T(8,128)(2,1)S(1)} %broadcast_select_fusion.1), channel_id=1, source_target_pairs={{0,16},{1,17},{2,18},{3,19},{4,20},{5,21},{6,22},{7,23},{8,24},{9,... | collective-permute-start | bytes 1966088 | tf_op jit(solution)/shard_map/ppermute | solution.py:102
  175.1 38.4 %collective-permute-start = (s32[3]{0:T(128)S(1)}, s32[3]{0:T(128)S(1)}, u32[]{:S(2)}, u32[]{:S(2)}) collective-permute-start(s32[3]{0:T(128)S(1)} %pad_add_fusion.1), channel_id=1, source_target_pairs={{8,0},{12,4},{16,8},{20,12},{24,16},{28,20},{32,24},{36,28},{40,32... | collective-permute-start | bytes 44 | tf_op jit(solution)/shard_map/ppermute | solution.py:18
  180.5 33.0 %collective-permute-start.2 = (s32[3]{0:T(128)S(1)}, s32[3]{0:T(128)S(1)}, u32[]{:S(2)}, u32[]{:S(2)}) collective-permute-start(s32[3]{0:T(128)S(1)} %pad_add_fusion.2), channel_id=1, source_target_pairs={{4,0},{8,4},{12,8},{16,12},{20,16},{24,20},{28,24},{32,28},{36,32}... | collective-permute-start | bytes 44 | tf_op jit(solution)/shard_map/ppermute | solution.py:18
  186.7 13.1 %collective-permute-start.11 = (bf16[2,128,1280]{2,1,0:T(8,128)(2,1)S(1)}, bf16[2,128,1280]{2,1,0:T(8,128)(2,1)S(1)}, u32[]{:S(2)}, u32[]{:S(2)}) collective-permute-start(bf16[2,128,1280]{2,1,0:T(8,128)(2,1)S(1)} %broadcast_select_fusion.2), channel_id=1, source_target_pairs={{0,8},{1,9},{2,10},{3,11},{4,12},{5,13},{6,14},{7,15},{8,0},{9,1},... | collective-permute-start | bytes 1966088 | tf_op jit(solution)/shard_map/ppermute | solution.py:102
  190.4 44.4 %collective-permute-start.4 = (s32[3]{0:T(128)S(1)}, s32[3]{0:T(128)S(1)}, u32[]{:S(2)}, u32[]{:S(2)}) collective-permute-start(s32[3]{0:T(128)S(1)} %pad_add_fusion.3), channel_id=1, source_target_pairs={{0,4},{4,8},{8,12},{12,16},{16,20},{20,24},{24,28},{28,32},{32,36}... | collective-permute-start | bytes 44 | tf_op jit(solution)/shard_map/ppermute | solution.py:18
  200.0 8.1 %collective-permute-start.12 = (bf16[2,128,1280]{2,1,0:T(8,128)(2,1)S(1)}, bf16[2,128,1280]{2,1,0:T(8,128)(2,1)S(1)}, u32[]{:S(2)}, u32[]{:S(2)}) collective-permute-start(bf16[2,128,1280]{2,1,0:T(8,128)(2,1)S(1)} %broadcast_select_fusion.3), channel_id=1, source_target_pairs={{0,4},{1,5},{2,6},{3,7},{4,0},{5,1},{6,2},{7,3},{8,12},{9,13},{10,... | collective-permute-start | bytes 1966088 | tf_op jit(solution)/shard_map/ppermute | solution.py:102
  202.8 32.1 %collective-permute-start.6 = (s32[3]{0:T(128)S(1)}, s32[3]{0:T(128)S(1)}, u32[]{:S(2)}, u32[]{:S(2)}) collective-permute-start(s32[3]{0:T(128)S(1)} %pad_add_fusion.4), channel_id=1, source_target_pairs={{0,8},{4,12},{8,16},{12,20},{16,24},{20,28},{24,32},{28,36},{32,40... | collective-permute-start | bytes 44 | tf_op jit(solution)/shard_map/ppermute | solution.py:18
  208.3 24.8 %collective-permute-start.13 = (bf16[2,128,1280]{2,1,0:T(8,128)(2,1)S(1)}, bf16[2,128,1280]{2,1,0:T(8,128)(2,1)S(1)}, u32[]{:S(2)}, u32[]{:S(2)}) collective-permute-start(bf16[2,128,1280]{2,1,0:T(8,128)(2,1)S(1)} %broadcast_select_fusion.4), channel_id=1, source_target_pairs={{0,2},{1,3},{2,0},{3,1},{4,6},{5,7},{6,4},{7,5},{8,10},{9,11},{10,... | collective-permute-start | bytes 1966088 | tf_op jit(solution)/shard_map/ppermute | solution.py:102
  233.2 31.0 %collective-permute-start.14 = (bf16[2,128,1280]{2,1,0:T(8,128)(2,1)S(1)}, bf16[2,128,1280]{2,1,0:T(8,128)(2,1)S(1)}, u32[]{:S(2)}, u32[]{:S(2)}) collective-permute-start(bf16[2,128,1280]{2,1,0:T(8,128)(2,1)S(1)} %broadcast_select_fusion.5), channel_id=1, source_target_pairs={{0,1},{1,0},{2,3},{3,2},{4,5},{5,4},{6,7},{7,6},{8,9},{9,8},{10,11... | collective-permute-start | bytes 1966088 | tf_op jit(solution)/shard_map/ppermute | solution.py:102
  269.1 47.9 %collective-permute-start.1 = (bf16[3,128,2560]{2,1,0:T(8,128)(2,1)}, bf16[3,128,2560]{2,1,0:T(8,128)(2,1)}, u32[]{:S(2)}, u32[]{:S(2)}) collective-permute-start(bf16[3,128,2560]{2,1,0:T(8,128)(2,1)} %gather_fusion.4), channel_id=1, source_target_pairs={{0,8},{4,12},{8,16},{12,20},{16,24},{20,28},{24,32},{28,36},{32,40... | collective-permute-start | bytes 5898248 | tf_op jit(solution)/shard_map/ppermute | solution.py:18
  276.7 58.5 %collective-permute-start.3 = (bf16[3,128,2560]{2,1,0:T(8,128)(2,1)}, bf16[3,128,2560]{2,1,0:T(8,128)(2,1)}, u32[]{:S(2)}, u32[]{:S(2)}) collective-permute-start(bf16[3,128,2560]{2,1,0:T(8,128)(2,1)} %gather_fusion.5), channel_id=1, source_target_pairs={{0,4},{4,8},{8,12},{12,16},{16,20},{20,24},{24,28},{28,32},{32,36}... | collective-permute-start | bytes 5898248 | tf_op jit(solution)/shard_map/ppermute | solution.py:18
  283.2 53.7 %collective-permute-start.5 = (bf16[3,128,2560]{2,1,0:T(8,128)(2,1)}, bf16[3,128,2560]{2,1,0:T(8,128)(2,1)}, u32[]{:S(2)}, u32[]{:S(2)}) collective-permute-start(bf16[3,128,2560]{2,1,0:T(8,128)(2,1)} %gather_fusion.6), channel_id=1, source_target_pairs={{4,0},{8,4},{12,8},{16,12},{20,16},{24,20},{28,24},{32,28},{36,32}... | collective-permute-start | bytes 5898248 | tf_op jit(solution)/shard_map/ppermute | solution.py:18
  287.3 12.8 %slice-start = ((s8[5242880]{0:T(1024)(128)(4,1)}), s8[1048576]{0:T(1024)(128)(4,1)S(1)}, s32[]{:S(2)}) async-start(s8[5242880]{0:T(1024)(128)(4,1)} %bitcast.185), calls=%async_computation.3 | async-start | bytes 2097152
  292.0 8.1 %slice-start.1 = ((s8[5242880]{0:T(1024)(128)(4,1)}), s8[4194304]{0:T(1024)(128)(4,1)S(1)}, s32[]{:S(2)}) async-start(s8[5242880]{0:T(1024)(128)(4,1)} %bitcast.185), calls=%async_computation.4 | async-start | bytes 8388608
  292.0 61.8 %collective-permute-start.7 = (bf16[3,128,2560]{2,1,0:T(8,128)(2,1)}, bf16[3,128,2560]{2,1,0:T(8,128)(2,1)S(1)}, u32[]{:S(2)}, u32[]{:S(2)}) collective-permute-start(bf16[3,128,2560]{2,1,0:T(8,128)(2,1)} %gather_fusion.7), channel_id=1, source_target_pairs={{8,0},{12,4},{16,8},{20,12},{24,16},{28,20},{32,24},{36,28},{40,32... | collective-permute-start | bytes 5898248 | tf_op jit(solution)/shard_map/ppermute | solution.py:18
  338.5 20.6 %slice-start.2 = ((bf16[256,3840]{1,0:T(8,128)(2,1)}), bf16[256,1280]{1,0:T(8,128)(2,1)S(1)}, s32[]{:S(2)}) async-start(bf16[256,3840]{1,0:T(8,128)(2,1)} %copy-done.4), calls=%async_computation.5 | async-start | bytes 1310720 | tf_op jit(solution)/shard_map/slice | solution.py:113
  338.5 20.6 %copy-start.11 = (bf16[2,128,1280]{2,1,0:T(8,128)(2,1)S(1)}, bf16[2,128,1280]{2,1,0:T(8,128)(2,1)}, u32[]{:S(2)}) copy-start(bf16[2,128,1280]{2,1,0:T(8,128)(2,1)} %custom-call.17) | copy-start | bytes 1966084
  338.6 20.6 %copy-start.12 = (s32[2]{0:T(128)S(1)}, s32[2]{0:T(128)}, u32[]{:S(2)}) copy-start(s32[2]{0:T(128)} %param.16) | copy-start | bytes 28
  354.1 5.0 %copy-start.2 = (bf16[22,128,2560]{2,1,0:T(8,128)(2,1)}, bf16[22,128,2560]{2,1,0:T(8,128)(2,1)S(1)}, u32[]{:S(2)}) copy-start(bf16[22,128,2560]{2,1,0:T(8,128)(2,1)S(1)} %constant_dynamic-update-slice_fusion.1) | copy-start | bytes 43253764
  486.0 3.9 copy-start.1
  (2 other events, 2.5 us)
Sparse Core Ops, SparseCore 0:
  134.4 58.4 all-gather.2
  208.2 61.5 all-gather.4
